TPU v7x, 128 devices: a whole 4x4x4 slice. The times are simulated.
128 devices in a mesh: runs: 32 (over x, z, y_hi), chan: 4 (over y_lo, core).
Axes of the slice: x: 4, y: 4 (y_hi: 2, y_lo: 2; y = y_hi * 2 + y_lo), z: 4, core: 2. Of those that a mesh axis runs over, the one named last changes fastest.
Arguments:
- slices: bfloat16 [256, 512, 8192], P('runs', None, 'chan'), may hold values from -6 to 6
- spectra: bfloat16 [2, 48, 8192], P(None, None, 'chan'), may hold values from -0.0625 to 0.0625
- loadings: float32 [256, 48], replicated, may hold values from 0.5 to 2
- mixing: float32 [2, 48, 48], replicated, may hold values from -1 to 3.5
- halves: int32 [256], replicated, may hold values from 0 to 1, as said below
- partner: int32 [256], replicated, may hold values from 0 to 255, as said below
Outputs:
- new_spectra: float32 [2, 48, 8192], P(None, None, 'chan')
- held_residual: float32 [256, 48, 8192], P('runs', None, 'chan')
Inputs may be any that keep to these rules, and one draw needn't show every extreme that they name: `halves`: exactly half of the 256 runs are in each half. partner pairs every run with a run of the other half, and the partner of a run's partner is the run itself.
All inputs are finite; a program needn't handle non-finite values.
Results may differ from a plain program's by a relative error of at most 0.0045.
Values may be sent and summed in bfloat16 or wider, within the bound.
No kernel may reach another device: no remote copies, remote signals or barrier semaphores. Data moves between devices by JAX's collectives and lax.ppermute only.
A program may use at most 64 MiB of HBM per device.

v0:
```python
import jax
import jax.numpy as jnp
from jax import lax
from jax.sharding import PartitionSpec as P

NS_STEPS = 10


def polar_scale(gram):
    eye_rank = jnp.eye(gram.shape[-1], dtype=jnp.float32)
    traces = jnp.trace(gram, axis1=1, axis2=2)
    start = eye_rank[None] / jnp.sqrt(traces + 1e-06)[:, None, None]

    def advance(step, factor):
        left = jnp.einsum("nrs,nrt->nst", factor, gram, precision=lax.Precision.HIGHEST)
        inner = jnp.einsum("nst,ntu->nsu", left, factor, precision=lax.Precision.HIGHEST)
        return 0.5 * jnp.einsum(
            "nrs,nsu->nru", factor, 3.0 * eye_rank[None] - inner, precision=lax.Precision.HIGHEST
        )

    return lax.fori_loop(0, NS_STEPS, advance, start)


def project(slices, rows_low, mixed):
    partial_basis = jnp.einsum("nrj,nij->nri", rows_low, slices, preferred_element_type=jnp.float32)
    basis = lax.psum(partial_basis, "chan")
    scaled = jnp.einsum("nrs,nsi->nri", mixed, basis, precision=lax.Precision.HIGHEST)
    gram = jnp.einsum("nri,nsi->nrs", scaled, scaled, precision=lax.Precision.HIGHEST)
    factor = polar_scale(gram)
    rotated = jnp.einsum("nrs,nri->nsi", factor, scaled, precision=lax.Precision.HIGHEST).astype(
        jnp.bfloat16
    )
    result = jnp.einsum("nsi,nij->nsj", rotated, slices, preferred_element_type=jnp.float32)
    return result


def solve_one(lower, target):
    return jax.scipy.linalg.cho_solve((lower, True), target)


def solve_halves(system, moments):
    lower = jnp.linalg.cholesky(system)
    return jax.vmap(solve_one)(lower, moments)


def body(slices, spectra, loadings, mixing, halves, partner):
    run_count = slices.shape[0]
    total_runs = loadings.shape[0]
    first_run = lax.axis_index("runs") * run_count
    mine = first_run + jnp.arange(run_count, dtype=jnp.int32)
    all_runs = jnp.arange(total_runs, dtype=jnp.int32)
    matches = all_runs[None, :] == mine[:, None]
    my_halves = jnp.sum(jnp.where(matches, halves[None, :], 0), axis=1)
    my_mates = jnp.sum(jnp.where(matches, partner[None, :], 0), axis=1)
    my_loads = jnp.dot(matches.astype(jnp.float32), loadings, precision=lax.Precision.HIGHEST)
    mate_match = (all_runs[None, :] == my_mates[:, None]).astype(jnp.float32)
    mate_loads = jnp.dot(mate_match, loadings, precision=lax.Precision.HIGHEST)
    first_half = (my_halves == 0)[:, None, None]
    own_rows = jnp.where(first_half, spectra[0][None], spectra[1][None])
    own_mix = jnp.where(first_half, mixing[0][None], mixing[1][None]) * my_loads[:, None, :]
    projected = project(slices, own_rows, own_mix)
    terms = jnp.einsum("nsr,nsj->nrj", own_mix, projected, precision=lax.Precision.HIGHEST)
    mine_member = (my_halves[:, None] == jnp.arange(2, dtype=jnp.int32)[None, :]).astype(
        jnp.float32
    )
    partial_moments = jnp.einsum("nh,nrj->hrj", mine_member, terms, precision=lax.Precision.HIGHEST)
    member = (halves[:, None] == jnp.arange(2, dtype=jnp.int32)[None, :]).astype(jnp.float32)
    cross = jnp.einsum("kh,kr,ks->hrs", member, loadings, loadings, precision=lax.Precision.HIGHEST)
    inner_mix = jnp.einsum("hsr,hst->hrt", mixing, mixing, precision=lax.Precision.HIGHEST)
    system = inner_mix * cross
    moments = lax.psum(partial_moments, "runs")
    new_spectra = solve_halves(system, moments)
    held_rows = jnp.where(first_half, new_spectra[1][None], new_spectra[0][None])
    held_mix = jnp.where(first_half, mixing[1][None], mixing[0][None]) * mate_loads[:, None, :]
    held_projected = project(slices, held_rows.astype(jnp.bfloat16), held_mix)
    model_part = jnp.einsum("nrs,nsj->nrj", held_mix, held_rows, precision=lax.Precision.HIGHEST)
    return (new_spectra, held_projected - model_part)


def solution(mesh):
    placed = (P("runs", None, "chan"), P(None, None, "chan"), P(), P(), P(), P())
    return jax.shard_map(
        body,
        mesh=mesh,
        in_specs=placed,
        out_specs=(P(None, None, "chan"), P("runs", None, "chan")),
        check_vma=False,
    )
```

profile of v0, /device:TPU:1, one launch (start us, length us, event | category | flops | bytes accessed | tf_op | source)
XLA Modules:
  0.0 539.7 jit_solution(11662439572653921339)
XLA Ops:
  7.2 0.9 select_reduce_fusion.3
  8.1 1.1 slice_bitcast_fusion.3
  9.2 11.9 %fusion.17 = f32[8,48,512]{2,1,0:T(8,128)} fusion(bf16[8,512,2048]{2,1,0:T(8,128)(2,1)} %param.10, pred[8]{0:T(512)(128)(4,1)S(1)} %broadcast_compare_fusion, bf16[48,2048]{1,0:T(8,128)(2,1)S(1)} %get-tuple-element.81, bf16[48,2048]{1,0:T(8,128)(2,1)S(1)} %get-tuple-element.80), kind=kOutput, calls=%fused_computation.23 | convolution fusion | flops 806092800 | bytes 17956872 | tf_op jit(solution)/shard_map/nrj,nij->nri/dot_general | solution.py:25
  22.1 42.1 %all-reduce.4.cloned.1.call-done = f32[8,48,512]{2,1,0:T(8,128)} async-done(((f32[8,48,512]{2,1,0:T(8,128)}), f32[8,48,512]{2,1,0:T(8,128)}) %all-reduce.4.cloned.1.call-update) | async-done | bytes 786448 | tf_op jit(solution)/shard_map/psum | solution.py:26
  64.3 2.0 fusion.26
  66.2 0.9 select_reduce_fusion.1
  67.3 11.6 %while.22 = (s32[]{:T(128)}, f32[8,48,48]{1,2,0:T(8,128)S(1)}, f32[8,48,48]{2,1,0:T(8,128)S(1)}, s32[]{:T(128)}) while((s32[]{:T(128)}, f32[8,48,48]{1,2,0:T(8,128)S(1)}, f32[8,48,48]{2,1,0:T(8,128)S(1)}, s32[]{:T(128)}) %tuple.47), condition=%wide.region_6.7_spmd.clone, body=%wide.region_5.6_spmd.clone.sunk | while | flops 31891968 | bytes 829493 | solution.py:21
  67.5 0.3 fusion.126
  67.8 0.4 convolution_subtract_fusion.5
  68.6 0.3 fusion.126
  69.0 0.4 convolution_subtract_fusion.5
  69.8 0.3 fusion.126
  70.1 0.4 convolution_subtract_fusion.5
  70.9 0.3 fusion.126
  71.3 0.4 convolution_subtract_fusion.5
  72.1 0.3 fusion.126
  72.4 0.4 convolution_subtract_fusion.5
  73.2 0.3 fusion.126
  73.6 0.4 convolution_subtract_fusion.5
  74.4 0.3 fusion.126
  74.7 0.4 convolution_subtract_fusion.5
  75.5 0.3 fusion.126
  75.8 0.4 convolution_subtract_fusion.5
  76.6 0.3 fusion.126
  77.0 0.4 convolution_subtract_fusion.5
  77.8 0.3 fusion.126
  78.1 0.4 convolution_subtract_fusion.5
  78.9 0.8 convolution_convert_fusion.1
  79.7 8.8 %fusion.66 = f32[8,48,2048]{2,1,0:T(8,128)S(1)} fusion(bf16[8,48,512]{2,1,0:T(8,128)(2,1)S(1)} %convolution_convert_fusion.1, bf16[8,512,2048]{2,1,0:T(8,128)(2,1)} %param.10), kind=kOutput, calls=%fused_computation.102 | convolution fusion | flops 805306368 | bytes 20316160 | tf_op jit(solution)/shard_map/nsi,nij->nsj/dot_general | solution.py:33
  88.5 3.1 fusion.25
  91.6 3.3 fusion.10
  94.9 1.3 copy.24
  96.4 9.0 %custom-call.11 = f32[2,48,48]{2,1,0:T(8,128)S(1)} custom-call(f32[2,48,48]{2,1,0:T(8,128)S(1)} %fusion.51), custom_call_target="Cholesky" | custom-call | tf_op jit(solution)/shard_map/jit(cholesky)/cholesky | solution.py:42
  105.6 7.4 %custom-call.12 = f32[2,1,48,48]{2,3,1,0:T(8,128)S(1)} custom-call(f32[2,1,48,48]{3,2,1,0:T(8,128)S(1)} %select_bitcast_fusion), custom_call_target="InvertDiagBlocksLowerTriangular" | custom-call | tf_op jit(solution)/shard_map/vmap(jit(_cho_solve))/triangular_solve | solution.py:38
  113.0 315.1 %all-reduce.6.cloned.1.call-done = f32[2,48,2048]{2,1,0:T(8,128)} async-done(((f32[2,48,2048]{2,1,0:T(8,128)}), f32[2,48,2048]{2,1,0:T(8,128)}) %all-reduce.6.cloned.1.call-update) | async-done | bytes 786448 | tf_op jit(solution)/shard_map/psum | solution.py:71
  428.1 2.0 fusion.48
  430.1 0.8 fusion.46
  431.0 12.1 %fusion.12 = f32[8,48,512]{2,1,0:T(8,128)} fusion(bf16[8,512,2048]{2,1,0:T(8,128)(2,1)} %param.10, f32[48,2048]{1,0:T(8,128)S(1)} %get-tuple-element.79, f32[48,2048]{1,0:T(8,128)S(1)} %get-tuple-element.78, pred[8]{0:T(512)(128)(4,1)S(1)} %broadcast_compare_fusion), kind=kOutput, calls=%fused_computation.18 | convolution fusion | flops 806092800 | bytes 18350088 | tf_op jit(solution)/shard_map/nrj,nij->nri/dot_general | solution.py:25
  443.2 4.5 fusion.8
  447.7 58.4 %all-reduce.8.cloned.1.call-done = f32[8,48,512]{2,1,0:T(8,128)} async-done(((f32[8,48,512]{2,1,0:T(8,128)}), f32[8,48,512]{2,1,0:T(8,128)}) %all-reduce.8.cloned.1.call-update) | async-done | bytes 786448 | tf_op jit(solution)/shard_map/psum | solution.py:26
  506.1 2.0 fusion.24
  508.1 0.9 select_reduce_fusion
  509.2 11.7 %while.23 = (s32[]{:T(128)}, f32[8,48,48]{1,2,0:T(8,128)S(1)}, f32[8,48,48]{2,1,0:T(8,128)S(1)}, s32[]{:T(128)}) while((s32[]{:T(128)}, f32[8,48,48]{1,2,0:T(8,128)S(1)}, f32[8,48,48]{2,1,0:T(8,128)S(1)}, s32[]{:T(128)}) %tuple.50), condition=%wide.region_12.13_spmd.clone, body=%wide.region_11.12_spmd.clone.sunk | while | flops 31891968 | bytes 829493 | solution.py:21
  509.2 0.3 fusion.135
  509.5 0.4 convolution_subtract_fusion.6
  510.3 0.3 fusion.135
  510.7 0.4 convolution_subtract_fusion.6
  511.5 0.3 fusion.135
  511.8 0.4 convolution_subtract_fusion.6
  512.6 0.3 fusion.135
  513.0 0.4 convolution_subtract_fusion.6
  513.8 0.3 fusion.135
  514.1 0.4 convolution_subtract_fusion.6
  514.9 0.3 fusion.135
  515.3 0.4 convolution_subtract_fusion.6
  516.1 0.3 fusion.135
  516.4 0.4 convolution_subtract_fusion.6
  517.2 0.3 fusion.135
  517.6 0.4 convolution_subtract_fusion.6
  518.4 0.3 fusion.135
  518.7 0.4 convolution_subtract_fusion.6
  519.8 0.4 convolution_subtract_fusion.6
  520.9 0.8 convolution_convert_fusion
  521.7 11.5 %convolution_subtract_fusion.2 = f32[8,48,2048]{2,1,0:T(8,128)} fusion(f32[8,48,2048]{2,1,0:T(8,128)} %fusion.8, bf16[8,48,512]{2,1,0:T(8,128)(2,1)S(1)} %convolution_convert_fusion, bf16[8,512,2048]{2,1,0:T(8,128)(2,1)} %param.10), kind=kOutput, calls=%fused_computation.17 | convolution fusion | flops 806092800 | bytes 23461888 | tf_op jit(solution)/shard_map/nsi,nij->nsj/dot_general | solution.py:33
  (98 shorter events, 8.9 us)
Async XLA Ops:
  7.2 57.1 %all-reduce.4.cloned.1.call-start = ((), (), s32[]{:S(2)}) async-start(), calls=%async_computation | async-start | bytes 1572864 | tf_op jit(solution)/shard_map/psum | solution.py:26
  9.2 12.0 %copy-start.3 = (s32[256]{0:T(256)S(1)}, s32[256]{0:T(256)}, u32[]{:S(2)}) copy-start(s32[256]{0:T(256)} %param.14) | copy-start | bytes 3076
  9.2 12.1 %copy-start.2 = (f32[256,48]{0,1:T(8,128)S(1)}, f32[256,48]{0,1:T(8,128)}, u32[]{:S(2)}) copy-start(f32[256,48]{0,1:T(8,128)} %param.12) | copy-start | bytes 147460
  9.2 12.4 %copy-start.1 = (f32[2,48,48]{2,1,0:T(8,128)S(1)}, f32[2,48,48]{2,1,0:T(8,128)}, u32[]{:S(2)}) copy-start(f32[2,48,48]{2,1,0:T(8,128)} %param.13) | copy-start | bytes 55300
  21.1 407.0 %all-reduce.6.cloned.1.call-start = ((), (), s32[]{:S(2)}) async-start(), calls=%async_computation.1 | async-start | bytes 1572864 | tf_op jit(solution)/shard_map/psum | solution.py:71
  96.3 409.9 %all-reduce.8.cloned.1.call-start = ((), (), s32[]{:S(2)}) async-start(), calls=%async_computation.2 | async-start | bytes 1572864 | tf_op jit(solution)/shard_map/psum | solution.py:26
  430.9 12.1 %copy-start = (f32[2,48,2048]{2,1,0:T(8,128)}, f32[2,48,2048]{2,1,0:T(8,128)S(1)}, u32[]{:S(2)}) copy-start(f32[2,48,2048]{2,1,0:T(8,128)S(1)} %fusion.46) | copy-start | bytes 2359300
Sparse Core Ops, SparseCore 0:
  21.2 42.9 all-reduce.3
  96.4 331.6 all-reduce.5
  443.2 62.9 all-reduce.7
where the time goes:
time: 540 us
  waiting for transfers between devices  416 us (77%)
  matrix products  87.5 us (16%)
  other arithmetic  17.9 us (3%)
  between operations  14 us (3%)
    psum x1, waiting for transfers between devices, body(): moments = lax.psum(partial_moments, 'runs')  315 us
    psum x2, waiting for transfers between devices, project(): basis = lax.psum(partial_basis, 'chan')  101 us
    dot_general x2, matrix products, project(): jnp.einsum('nrj,nij->nri', rows_low, slices, preferred_element_type=jnp.f...  23.9 us
    dot_general x2, matrix products, project(): jnp.einsum('nsi,nij->nsj', rotated, slices, preferred_element_type=jnp.fl...  20.3 us
  transfers between devices with their start and end apart: 3, of which 3 were waited for; matrix products, arithmetic and copies ran while one was open for 4% of the time, Pallas kernels for 0%

commit v1 on v0

--- a/solution.py
+++ b/solution.py
@@ -68,7 +68,7 @@
     cross = jnp.einsum("kh,kr,ks->hrs", member, loadings, loadings, precision=lax.Precision.HIGHEST)
     inner_mix = jnp.einsum("hsr,hst->hrt", mixing, mixing, precision=lax.Precision.HIGHEST)
     system = inner_mix * cross
-    moments = lax.psum(partial_moments, "runs")
+    moments = jnp.sum(lax.all_gather(partial_moments, "runs"), axis=0)
     new_spectra = solve_halves(system, moments)
     held_rows = jnp.where(first_half, new_spectra[1][None], new_spectra[0][None])
     held_mix = jnp.where(first_half, mixing[1][None], mixing[0][None]) * mate_loads[:, None, :]

time: 540 us -> 402 us (0.74)
  waiting for transfers between devices: 416 us -> 266 us
  other arithmetic: 17.9 us -> 27 us
    psum x1 -> x0, waiting for transfers between devices: 315 us -> none  [body(): moments = lax.psum(partial_moments, 'runs')]
    all_gather x0 -> x1, waiting for transfers between devices: none -> 189 us  [body(): moments = jnp.sum(lax.all_gather(partial_moments, 'runs'), axis=0)]
    psum x2, waiting for transfers between devices: 101 us -> 76.6 us  [project(): basis = lax.psum(partial_basis, 'chan')]
    reduce_sum x0 -> x1, other arithmetic: none -> 9.05 us  [body(): moments = jnp.sum(lax.all_gather(partial_moments, 'runs'), axis=0)]
  transfers between devices with their start and end apart: 3 -> 3, of which waited for: 3 -> 3; matrix products, arithmetic and copies ran while one was open for 4% -> 6% of each run, Pallas kernels for 0% -> 0%
where the time goes in v1:
time: 402 us
  waiting for transfers between devices  266 us (66%)
  matrix products  89.9 us (22%)
  other arithmetic  27 us (7%)
  between operations  14 us (3%)
    all_gather x1, waiting for transfers between devices, body(): moments = jnp.sum(lax.all_gather(partial_moments, 'runs'), axis=0)  189 us
    psum x2, waiting for transfers between devices, project(): basis = lax.psum(partial_basis, 'chan')  76.6 us
    dot_general x2, matrix products, project(): jnp.einsum('nrj,nij->nri', rows_low, slices, preferred_element_type=jnp.f...  23.9 us
    dot_general x2, matrix products, project(): jnp.einsum('nsi,nij->nsj', rotated, slices, preferred_element_type=jnp.fl...  20.3 us
    dot_general x20, matrix products, advance(): jnp.einsum('nrs,nsu->nru', factor, 3.0 * eye_rank[None] - inner, precisio...  9.94 us
    another operation x4, other arithmetic, solve_halves(): lower = jnp.linalg.cholesky(system)  9.19 us
    reduce_sum x1, other arithmetic, body(): moments = jnp.sum(lax.all_gather(partial_moments, 'runs'), axis=0)  9.05 us
    dot_general x20, matrix products, advance(): jnp.einsum('nst,ntu->nsu', left, factor, precision=lax.Precision.HIGHEST)  8.73 us
  transfers between devices with their start and end apart: 3, of which 3 were waited for; matrix products, arithmetic and copies ran while one was open for 6% of the time, Pallas kernels for 0%

profile of v1, /device:TPU:1, one launch (start us, length us, event | category | flops | bytes accessed | tf_op | source)
XLA Modules:
  0.0 401.5 jit_solution(11531501587760731275)
XLA Ops:
  7.2 0.9 select_reduce_fusion.3
  8.1 1.1 slice_bitcast_fusion.3
  9.2 11.8 %fusion.17 = f32[8,48,512]{2,1,0:T(8,128)} fusion(bf16[8,512,2048]{2,1,0:T(8,128)(2,1)} %param.10, pred[8]{0:T(512)(128)(4,1)S(1)} %broadcast_compare_fusion, bf16[48,2048]{1,0:T(8,128)(2,1)S(1)} %get-tuple-element.81, bf16[48,2048]{1,0:T(8,128)(2,1)S(1)} %get-tuple-element.80), kind=kOutput, calls=%fused_computation.23 | convolution fusion | flops 806092800 | bytes 17956872 | tf_op jit(solution)/shard_map/nrj,nij->nri/dot_general | solution.py:25
  21.5 42.8 %all-reduce.3.cloned.1.call-done = f32[8,48,512]{2,1,0:T(8,128)} async-done(((f32[8,48,512]{2,1,0:T(8,128)}), f32[8,48,512]{2,1,0:T(8,128)}) %all-reduce.3.cloned.1.call-update) | async-done | bytes 786448 | tf_op jit(solution)/shard_map/psum | solution.py:26
  64.2 2.0 fusion.26
  66.2 0.9 select_reduce_fusion.1
  67.3 13.5 %while.22 = (s32[]{:T(128)}, f32[8,48,48]{1,2,0:T(8,128)S(1)}, f32[8,48,48]{2,1,0:T(8,128)S(1)}, s32[]{:T(128)}) while((s32[]{:T(128)}, f32[8,48,48]{1,2,0:T(8,128)S(1)}, f32[8,48,48]{2,1,0:T(8,128)S(1)}, s32[]{:T(128)}) %tuple.47), condition=%wide.region_6.7_spmd.clone, body=%wide.region_5.6_spmd.clone.sunk | while | flops 31891968 | bytes 829493 | solution.py:21
  67.8 0.4 convolution_subtract_fusion.5
  68.3 0.5 fusion.129
  69.1 0.4 convolution_subtract_fusion.5
  69.6 0.5 fusion.129
  70.5 0.4 convolution_subtract_fusion.5
  70.9 0.5 fusion.129
  71.8 0.4 convolution_subtract_fusion.5
  72.2 0.5 fusion.129
  73.1 0.4 convolution_subtract_fusion.5
  73.6 0.5 fusion.129
  74.4 0.4 convolution_subtract_fusion.5
  74.9 0.5 fusion.129
  75.8 0.4 convolution_subtract_fusion.5
  76.2 0.5 fusion.129
  77.1 0.4 convolution_subtract_fusion.5
  77.5 0.5 fusion.129
  78.4 0.4 convolution_subtract_fusion.5
  78.9 0.5 fusion.129
  79.8 0.4 convolution_subtract_fusion.5
  80.2 0.5 fusion.129
  80.7 0.8 convolution_convert_fusion.1
  81.5 8.8 %fusion.67 = f32[8,48,2048]{2,1,0:T(8,128)S(1)} fusion(bf16[8,48,512]{2,1,0:T(8,128)(2,1)S(1)} %convolution_convert_fusion.1, bf16[8,512,2048]{2,1,0:T(8,128)(2,1)} %param.10), kind=kOutput, calls=%fused_computation.103 | convolution fusion | flops 805306368 | bytes 20316160 | tf_op jit(solution)/shard_map/nsi,nij->nsj/dot_general | solution.py:33
  90.3 3.1 fusion.25
  93.4 3.3 fusion.10
  96.7 1.3 copy.34
  98.8 9.0 %custom-call.11 = f32[2,48,48]{2,1,0:T(8,128)S(1)} custom-call(f32[2,48,48]{2,1,0:T(8,128)S(1)} %fusion.51), custom_call_target="Cholesky" | custom-call | tf_op jit(solution)/shard_map/jit(cholesky)/cholesky | solution.py:42
  108.0 7.4 %custom-call.12 = f32[2,1,48,48]{2,3,1,0:T(8,128)S(1)} custom-call(f32[2,1,48,48]{3,2,1,0:T(8,128)S(1)} %select_bitcast_fusion), custom_call_target="InvertDiagBlocksLowerTriangular" | custom-call | tf_op jit(solution)/shard_map/vmap(jit(_cho_solve))/triangular_solve | solution.py:38
  115.4 189.4 %all-gather.3.cloned.1.call-done = f32[64,48,2048]{2,1,0:T(8,128)} async-done(((f32[2,48,2048]{2,1,0:T(8,128)}), f32[64,48,2048]{2,1,0:T(8,128)}) %all-gather.3.cloned.1.call-update) | async-done | bytes 25165840 | tf_op jit(solution)/shard_map/all_gather | solution.py:71
  304.9 9.0 %reduce_sum.45 = f32[2,48,2048]{2,1,0:T(8,128)S(1)} reduce(f32[32,2,48,2048]{3,2,1,0:T(8,128)} %bitcast.108, f32[]{:T(128)} %constant.79.clone.1), dimensions={0}, to_apply=%region_7.8 | reduce | flops 6094848 | bytes 25952260 | tf_op jit(solution)/shard_map/reduce_sum | solution.py:71
  313.9 0.8 fusion.48
  314.7 0.8 fusion.46
  315.6 12.1 %fusion.12 = f32[8,48,512]{2,1,0:T(8,128)} fusion(bf16[8,512,2048]{2,1,0:T(8,128)(2,1)} %param.10, f32[48,2048]{1,0:T(8,128)S(1)} %get-tuple-element.79, f32[48,2048]{1,0:T(8,128)S(1)} %get-tuple-element.78, pred[8]{0:T(512)(128)(4,1)S(1)} %broadcast_compare_fusion), kind=kOutput, calls=%fused_computation.18 | convolution fusion | flops 806092800 | bytes 18350088 | tf_op jit(solution)/shard_map/nrj,nij->nri/dot_general | solution.py:25
  327.9 4.5 %fusion.8 = f32[8,48,2048]{2,1,0:T(8,128)} fusion(f32[48,2048]{1,0:T(8,128)S(1)} %get-tuple-element.79, f32[48,2048]{1,0:T(8,128)S(1)} %get-tuple-element.78, pred[8]{0:T(512)(128)(4,1)S(1)} %broadcast_compare_fusion, f32[8,48]{1,0:T(8,128)S(1)} %fusion.56, f32[48,48]{1,0:T(8,128)S(1)} %get-tuple-element.83, f32[48,48]{1,0:T(8,128)S(1)} %get-tuple-element.82), kind=kOutput, calls=%fused_computation.12 | convolution fusion | flops 453808128 | bytes 3952136 | tf_op jit(solution)/shard_map/nrs,nsj->nrj/dot_general | solution.py:76
  332.4 33.8 %all-reduce.5.cloned.1.call-done = f32[8,48,512]{2,1,0:T(8,128)} async-done(((f32[8,48,512]{2,1,0:T(8,128)}), f32[8,48,512]{2,1,0:T(8,128)}) %all-reduce.5.cloned.1.call-update) | async-done | bytes 786448 | tf_op jit(solution)/shard_map/psum | solution.py:26
  366.2 2.0 fusion.24
  368.1 0.9 select_reduce_fusion
  369.2 13.5 %while.23 = (s32[]{:T(128)}, f32[8,48,48]{1,2,0:T(8,128)S(1)}, f32[8,48,48]{2,1,0:T(8,128)S(1)}, s32[]{:T(128)}) while((s32[]{:T(128)}, f32[8,48,48]{1,2,0:T(8,128)S(1)}, f32[8,48,48]{2,1,0:T(8,128)S(1)}, s32[]{:T(128)}) %tuple.50), condition=%wide.region_12.13_spmd.clone, body=%wide.region_11.12_spmd.clone.sunk | while | flops 31891968 | bytes 829493 | solution.py:21
  369.8 0.4 convolution_subtract_fusion.6
  370.3 0.5 fusion.138
  371.6 0.5 fusion.138
  372.5 0.4 convolution_subtract_fusion.6
  372.9 0.5 fusion.138
  373.8 0.4 convolution_subtract_fusion.6
  374.2 0.5 fusion.138
  375.1 0.4 convolution_subtract_fusion.6
  375.6 0.5 fusion.138
  376.5 0.4 convolution_subtract_fusion.6
  376.9 0.5 fusion.138
  377.8 0.4 convolution_subtract_fusion.6
  378.2 0.5 fusion.138
  379.1 0.4 convolution_subtract_fusion.6
  379.6 0.5 fusion.138
  380.4 0.4 convolution_subtract_fusion.6
  380.9 0.5 fusion.138
  382.2 0.5 fusion.138
  382.7 0.8 convolution_convert_fusion
  383.5 11.5 %convolution_subtract_fusion.2 = f32[8,48,2048]{2,1,0:T(8,128)} fusion(f32[8,48,2048]{2,1,0:T(8,128)} %fusion.8, bf16[8,48,512]{2,1,0:T(8,128)(2,1)S(1)} %convolution_convert_fusion, bf16[8,512,2048]{2,1,0:T(8,128)(2,1)} %param.10), kind=kOutput, calls=%fused_computation.17 | convolution fusion | flops 806092800 | bytes 23461888 | tf_op jit(solution)/shard_map/nsi,nij->nsj/dot_general | solution.py:33
  (99 shorter events, 9.5 us)
Async XLA Ops:
  7.2 57.1 %all-reduce.3.cloned.1.call-start = ((), (), s32[]{:S(2)}) async-start(), calls=%async_computation | async-start | bytes 1572864 | tf_op jit(solution)/shard_map/psum | solution.py:26
  9.2 12.1 %copy-start.2 = (f32[256,48]{0,1:T(8,128)S(1)}, f32[256,48]{0,1:T(8,128)}, u32[]{:S(2)}) copy-start(f32[256,48]{0,1:T(8,128)} %param.12) | copy-start | bytes 147460
  9.2 12.2 %copy-start.1 = (f32[2,48,48]{2,1,0:T(8,128)S(1)}, f32[2,48,48]{2,1,0:T(8,128)}, u32[]{:S(2)}) copy-start(f32[2,48,48]{2,1,0:T(8,128)} %param.13) | copy-start | bytes 55300
  21.1 283.8 %all-gather.3.cloned.1.call-start = ((), (), s32[]{:S(2)}) async-start(), calls=%async_computation.2 | async-start | bytes 25952256 | tf_op jit(solution)/shard_map/all_gather | solution.py:71
  93.4 4.7 %copy-start.3 = (s32[256]{0:T(256)S(1)}, s32[256]{0:T(256)}, u32[]{:S(2)}) copy-start(s32[256]{0:T(256)} %param.14) | copy-start | bytes 3076
  98.0 268.1 %all-reduce.5.cloned.1.call-start = ((), (), s32[]{:S(2)}) async-start(), calls=%async_computation.1 | async-start | bytes 1572864 | tf_op jit(solution)/shard_map/psum | solution.py:26
  315.5 12.1 %copy-start = (f32[2,48,2048]{2,1,0:T(8,128)}, f32[2,48,2048]{2,1,0:T(8,128)S(1)}, u32[]{:S(2)}) copy-start(f32[2,48,2048]{2,1,0:T(8,128)S(1)} %fusion.46) | copy-start | bytes 2359300
Sparse Core Ops, SparseCore 0:
  21.2 42.9 all-reduce.2
  98.1 206.6 all-gather.2
  327.8 38.2 all-reduce.4
